TPU v7x, 512 devices: a whole 4x8x8 slice. The times are simulated.
512 devices in a mesh: section: 8 (over z), ctx: 8 (over y_hi, x), tp: 8 (over y_lo, core).
Axes of the slice: x: 4, y: 8 (y_hi: 2, y_lo: 4; y = y_hi * 4 + y_lo), z: 8, core: 2. Of those that a mesh axis runs over, the one named last changes fastest.
Arguments:
- block_order: int32 [16], replicated, may hold values from 0 to 15, each once
- plan: int32 [8], replicated, may hold values from 0 to 1
- q_box: bfloat16 [8, 2, 1408, 8192], P('section', None, 'ctx', 'tp'), may hold values from -8 to 8
- k_box: bfloat16 [8, 2, 1408, 1024], P('section', None, ('ctx', 'tp')), may hold values from -8 to 8
- v_box: bfloat16 [8, 2, 1408, 1024], P('section', None, ('ctx', 'tp')), may hold values from -6 to 6
- grad_out: bfloat16 [8, 1408, 8192], P('section', 'ctx', 'tp'), may hold values from -6 to 6
Outputs:
- attn_out: bfloat16 [8, 1408, 8192], P('section', 'ctx', 'tp')
- grad_q: bfloat16 [8, 1408, 8192], P('section', 'ctx', 'tp')
- grad_k: float32 [8, 1408, 1024], P('section', ('ctx', 'tp'))
- grad_v: float32 [8, 1408, 1024], P('section', ('ctx', 'tp'))
Inputs may be any that keep to these rules, and one draw needn't show every extreme that they name: `block_order`: a permutation: every block sits in exactly one storage slot, slot j covering storage rows j * 88 to (j + 1) * 88 - 1.
All inputs are finite; a program needn't handle non-finite values.
Results may differ from a plain program's by a relative error of at most 0.012.
Values may be sent and summed in bfloat16 or wider, within the bound.
No kernel may reach another device: no remote copies, remote signals or barrier semaphores. Data moves between devices by JAX's collectives and lax.ppermute only.
A program may use at most 64 MiB of HBM per device.

v0:
```python
import jax
import jax.numpy as jnp
from jax import lax
from jax.sharding import PartitionSpec as P

HEAD_DIM = 128
NEG = -1e30


def passed_along(block, axis, distance):
    devices = range(lax.axis_size(axis))
    route = [((i - distance) % len(devices), i) for i in devices]
    return lax.ppermute(block, axis, route)


def body(block_order, plan, q_box, k_box, v_box, grad_out):
    tp_count = lax.axis_size("tp")
    ctx_count = lax.axis_size("ctx")
    tok_rows = q_box.shape[2]
    seq_rows = tok_rows * ctx_count
    block_len = tok_rows // 2
    head_size = HEAD_DIM
    heads_local = q_box.shape[3] // head_size
    kv_local = k_box.shape[3] // head_size // tp_count
    group = heads_local // kv_local
    kv_width = kv_local * head_size
    scale = head_size ** (-0.5)
    section_rank = lax.axis_index("section")
    tp_rank = lax.axis_index("tp")
    arrived = passed_along((q_box[0], k_box[0], v_box[0]), "section", 1)
    wanted = lax.dynamic_index_in_dim(plan, section_rank, 0, keepdims=False)
    queries = lax.dynamic_index_in_dim(arrived[0], wanted, 0, keepdims=False)
    key_rows = lax.dynamic_index_in_dim(arrived[1], wanted, 0, keepdims=False)
    value_rows = lax.dynamic_index_in_dim(arrived[2], wanted, 0, keepdims=False)
    cotangent = passed_along(grad_out[0], "section", -1)
    positions = (
        block_order[:, None] * block_len + jnp.arange(block_len, dtype=jnp.int32)[None, :]
    ).reshape(seq_rows)
    query_pos = lax.dynamic_slice_in_dim(positions, lax.axis_index("ctx") * tok_rows, tok_rows)
    key_full, value_full = (
        lax.all_gather(key_rows, ("ctx", "tp"), axis=0, tiled=True),
        lax.all_gather(value_rows, ("ctx", "tp"), axis=0, tiled=True),
    )
    key_store = lax.dynamic_slice_in_dim(key_full, tp_rank * kv_width, kv_width, 1)
    value_store = lax.dynamic_slice_in_dim(value_full, tp_rank * kv_width, kv_width, 1)
    q_split = queries.reshape(tok_rows, kv_local, group, head_size).transpose(1, 2, 0, 3)
    do_split = cotangent.reshape(tok_rows, kv_local, group, head_size).transpose(1, 2, 0, 3)
    key_split = key_store.reshape(seq_rows, kv_local, head_size).transpose(1, 0, 2)
    value_split = value_store.reshape(seq_rows, kv_local, head_size).transpose(1, 0, 2)
    visible_all = positions[None, :] <= query_pos[:, None]

    def per_group(inputs):
        q_group, do_group, key_head, value_head = inputs

        def per_head(sums, head_inputs):
            key_grad, value_grad = sums
            q_one, do_one = head_inputs
            scores = jnp.dot(q_one, key_head.T, preferred_element_type=jnp.float32) * scale
            scores = jnp.where(visible_all, scores, NEG)
            top_score = jnp.max(scores, axis=1, keepdims=True)
            totals = jnp.sum(
                jnp.where(visible_all, jnp.exp(scores - top_score), 0.0), axis=1, keepdims=True
            )
            log_total = top_score + jnp.log(totals)
            probs = jnp.where(visible_all, jnp.exp(scores - log_total), 0.0)
            probs_low = probs.astype(jnp.bfloat16)
            attended = jnp.dot(probs_low, value_head, preferred_element_type=jnp.float32)
            delta = jnp.sum(do_one.astype(jnp.float32) * attended, axis=1, keepdims=True)
            dprobs = jnp.dot(do_one, value_head.T, preferred_element_type=jnp.float32)
            dscores = (probs * (dprobs - delta)).astype(jnp.bfloat16)
            q_grad = (
                jnp.dot(dscores, key_head, preferred_element_type=jnp.float32) * scale
            ).astype(jnp.bfloat16)
            key_grad = (
                key_grad + jnp.dot(dscores.T, q_one, preferred_element_type=jnp.float32) * scale
            )
            value_grad = value_grad + jnp.dot(
                probs_low.T, do_one, preferred_element_type=jnp.float32
            )
            return ((key_grad, value_grad), (attended.astype(jnp.bfloat16), q_grad))

        zero_rows = jnp.zeros((seq_rows, head_size), jnp.float32)
        (key_grad, value_grad), (attended, q_grad) = lax.scan(
            per_head, (zero_rows, zero_rows), (q_group, do_group)
        )
        return (attended, q_grad, key_grad, value_grad)

    attended, q_grad, key_grad, value_grad = lax.map(
        per_group, (q_split, do_split, key_split, value_split)
    )
    attended_flat = attended.transpose(2, 0, 1, 3).reshape(tok_rows, heads_local * head_size)
    q_grad_flat = q_grad.transpose(2, 0, 1, 3).reshape(tok_rows, heads_local * head_size)
    key_terms = key_grad.transpose(1, 0, 2).reshape(seq_rows, kv_width)
    value_terms = value_grad.transpose(1, 0, 2).reshape(seq_rows, kv_width)
    grad_terms = jnp.concatenate([key_terms, value_terms], axis=1)
    own_grads = lax.psum_scatter(grad_terms, "ctx", scatter_dimension=0, tiled=True)
    key_part = own_grads[:, :kv_width]
    value_part = own_grads[:, kv_width:]
    k_grad_tokens, v_grad_tokens = (
        lax.all_to_all(key_part, "tp", split_axis=0, concat_axis=1, tiled=True),
        lax.all_to_all(value_part, "tp", split_axis=0, concat_axis=1, tiled=True),
    )
    return (attended_flat[None], q_grad_flat[None], k_grad_tokens[None], v_grad_tokens[None])


def solution(mesh):
    in_specs = (
        P(),
        P(),
        P("section", None, "ctx", "tp"),
        P("section", None, ("ctx", "tp"), None),
        P("section", None, ("ctx", "tp"), None),
        P("section", "ctx", "tp"),
    )
    out_specs = (
        P("section", "ctx", "tp"),
        P("section", "ctx", "tp"),
        P("section", ("ctx", "tp"), None),
        P("section", ("ctx", "tp"), None),
    )
    return jax.shard_map(body, mesh=mesh, in_specs=in_specs, out_specs=out_specs, check_vma=False)
```

profile of v0, /device:TPU:1, one launch (start us, length us, event | category | flops | bytes accessed | tf_op | source)
XLA Modules:
  0.0 454.2 jit_solution(15236497514800470888)
XLA Ops:
  7.2 4.8 %collective-permute-start.3 = (bf16[2,22,1024]{2,0,1:T(2,128)(2,1)}, bf16[2,22,1024]{2,0,1:T(2,128)(2,1)S(1)}, u32[]{:S(2)}, u32[]{:S(2)}) collective-permute-start(bf16[2,22,1024]{2,0,1:T(2,128)(2,1)} %bitcast.117), channel_id=1, source_target_pairs={{448,0},{0,64},{64,128},{128,192},{192,256},{256,320},{320,384},{3... | collective-permute-start | bytes 270344 | tf_op jit(solution)/shard_map/ppermute | solution.py:13
  15.2 6.0 %collective-permute-done.3 = bf16[2,22,1024]{2,0,1:T(2,128)(2,1)S(1)} collective-permute-done((bf16[2,22,1024]{2,0,1:T(2,128)(2,1)}, bf16[2,22,1024]{2,0,1:T(2,128)(2,1)S(1)}, u32[]{:S(2)}, u32[]{:S(2)}) %collective-permute-start.3) | collective-permute-done | bytes 90144 | tf_op jit(solution)/shard_map/ppermute | solution.py:13
  22.0 1.9 collective-permute-start.1
  24.0 4.8 %collective-permute-done.1 = bf16[2,22,1024]{2,0,1:T(2,128)(2,1)S(1)} collective-permute-done((bf16[2,22,1024]{2,0,1:T(2,128)(2,1)}, bf16[2,22,1024]{2,0,1:T(2,128)(2,1)S(1)}, u32[]{:S(2)}, u32[]{:S(2)}) %collective-permute-start.1) | collective-permute-done | bytes 90144 | tf_op jit(solution)/shard_map/ppermute | solution.py:13
  29.5 1.9 collective-permute-start
  31.5 4.6 %collective-permute-start.2 = (bf16[176,1024]{1,0:T(8,128)(2,1)}, bf16[176,1024]{1,0:T(8,128)(2,1)S(1)}, u32[]{:S(2)}, u32[]{:S(2)}) collective-permute-start(bf16[176,1024]{1,0:T(8,128)(2,1)} %bitcast.116), channel_id=1, source_target_pairs={{64,0},{128,64},{192,128},{256,192},{320,256},{384,320},{448,384},... | collective-permute-start | bytes 1081352 | tf_op jit(solution)/shard_map/ppermute | solution.py:13
  37.0 4.4 collective-permute-done.2
  42.3 5.9 %collective-permute-done = bf16[2,176,1024]{2,1,0:T(8,128)(2,1)S(1)} collective-permute-done((bf16[2,176,1024]{2,1,0:T(8,128)(2,1)}, bf16[2,176,1024]{2,1,0:T(8,128)(2,1)S(1)}, u32[]{:S(2)}, u32[]{:S(2)}) %collective-permute-start) | collective-permute-done | bytes 720928 | tf_op jit(solution)/shard_map/ppermute | solution.py:13
  49.0 92.7 %all-gather.7.cloned.1.call-done = bf16[1,1408,1024]{2,0,1:T(2,128)(2,1)} async-done(((bf16[1,22,1024]{2,0,1:T(2,128)(2,1)}), bf16[1,1408,1024]{2,0,1:T(2,128)(2,1)}) %all-gather.7.cloned.1.call-update) | async-done | bytes 2883600 | tf_op jit(solution)/shard_map/all_gather | solution.py:42
  141.7 1.8 constant_dynamic-slice_fusion
  143.5 118.6 %all-gather.5.cloned.1.call-done = bf16[1,1408,1024]{2,0,1:T(2,128)(2,1)} async-done(((bf16[1,22,1024]{2,0,1:T(2,128)(2,1)}), bf16[1,1408,1024]{2,0,1:T(2,128)(2,1)}) %all-gather.5.cloned.1.call-update) | async-done | bytes 2883600 | tf_op jit(solution)/shard_map/all_gather | solution.py:41
  262.2 1.8 constant_dynamic-slice_fusion.2
  264.0 68.6 %while.30 = (s32[]{:T(128)}, f32[1408,128]{1,0:T(8,128)S(1)}, f32[1408,128]{1,0:T(8,128)S(1)}, bf16[8,176,128]{2,1,0:T(8,128)(2,1)}, bf16[8,176,128]{2,1,0:T(8,1...) while((s32[]{:T(128)}, f32[1408,128]{1,0:T(8,128)S(1)}, ...), condition=%wide.region_4.5_spmd.clone, body=%wide.region_0.4_spmd.clone.sunk | while | flops 386129568 | bytes 11705100 | solution.py:83
  276.8 1.4 fusion.65
  285.4 1.4 fusion.65
  294.0 1.4 fusion.65
  311.1 1.4 fusion.65
  319.7 1.4 fusion.65
  328.3 1.4 fusion.65
  333.8 89.6 %reduce-scatter.2.cloned.1.call-done = f32[176,256]{1,0:T(8,128)} async-done(((f32[1408,256]{1,0:T(8,128)}), f32[176,256]{1,0:T(8,128)}) %reduce-scatter.2.cloned.1.call-update) | async-done | bytes 180240 | tf_op jit(solution)/shard_map/reduce_scatter | solution.py:96
  425.0 7.0 %all-to-all-start = ((f32[8,22,128]{2,1,0:T(8,128)}), f32[8,22,128]{2,1,0:T(8,128)S(1)}, u32[]{:S(2)}, u32[]{:S(2)}) async-start(f32[8,22,128]{2,1,0:T(8,128)} %all_to_all.24), calls=%async_computation.1 | async-start | bytes 196608 | tf_op jit(solution)/shard_map/all_to_all | solution.py:100
  432.6 4.8 %all-to-all-done = f32[8,22,128]{2,1,0:T(8,128)S(1)} async-done(((f32[8,22,128]{2,1,0:T(8,128)}), f32[8,22,128]{2,1,0:T(8,128)S(1)}, u32[]{:S(2)}, u32[]{:S(2)}) %all-to-all-start) | async-done | bytes 90144 | tf_op jit(solution)/shard_map/all_to_all | solution.py:100
  437.4 4.2 all-to-all-start.1
  445.2 1.8 all-to-all-done.1
  (110 shorter events, 73.2 us)
Async XLA Ops:
  7.2 134.5 %all-gather.7.cloned.1.call-start = ((), (), s32[]{:S(2)}) async-start(), calls=%async_computation.5 | async-start | bytes 5857280 | tf_op jit(solution)/shard_map/all_gather | solution.py:42
  7.2 14.0 %collective-permute-start.3 = (bf16[2,22,1024]{2,0,1:T(2,128)(2,1)}, bf16[2,22,1024]{2,0,1:T(2,128)(2,1)S(1)}, u32[]{:S(2)}, u32[]{:S(2)}) collective-permute-start(bf16[2,22,1024]{2,0,1:T(2,128)(2,1)} %bitcast.117), channel_id=1, source_target_pairs={{448,0},{0,64},{64,128},{128,192},{192,256},{256,320},{320,384},{3... | collective-permute-start | bytes 270344 | tf_op jit(solution)/shard_map/ppermute | solution.py:13
  22.0 240.2 %all-gather.5.cloned.1.call-start = ((), (), s32[]{:S(2)}) async-start(), calls=%async_computation.4 | async-start | bytes 5857280 | tf_op jit(solution)/shard_map/all_gather | solution.py:41
  22.0 6.7 %collective-permute-start.1 = (bf16[2,22,1024]{2,0,1:T(2,128)(2,1)}, bf16[2,22,1024]{2,0,1:T(2,128)(2,1)S(1)}, u32[]{:S(2)}, u32[]{:S(2)}) collective-permute-start(bf16[2,22,1024]{2,0,1:T(2,128)(2,1)} %bitcast.118), channel_id=1, source_target_pairs={{448,0},{0,64},{64,128},{128,192},{192,256},{256,320},{320,384},{3... | collective-permute-start | bytes 270344 | tf_op jit(solution)/shard_map/ppermute | solution.py:13
  29.5 393.9 %reduce-scatter.2.cloned.1.call-start = ((), (), s32[]{:S(2)}) async-start(), calls=%async_computation.3 | async-start | bytes 1622016 | tf_op jit(solution)/shard_map/reduce_scatter | solution.py:96
  29.5 18.6 %collective-permute-start = (bf16[2,176,1024]{2,1,0:T(8,128)(2,1)}, bf16[2,176,1024]{2,1,0:T(8,128)(2,1)S(1)}, u32[]{:S(2)}, u32[]{:S(2)}) collective-permute-start(bf16[2,176,1024]{2,1,0:T(8,128)(2,1)} %bitcast.115), channel_id=1, source_target_pairs={{448,0},{0,64},{64,128},{128,192},{192,256},{256,320},{320,384},{3... | collective-permute-start | bytes 2162696 | tf_op jit(solution)/shard_map/ppermute | solution.py:13
  31.5 10.0 %collective-permute-start.2 = (bf16[176,1024]{1,0:T(8,128)(2,1)}, bf16[176,1024]{1,0:T(8,128)(2,1)S(1)}, u32[]{:S(2)}, u32[]{:S(2)}) collective-permute-start(bf16[176,1024]{1,0:T(8,128)(2,1)} %bitcast.116), channel_id=1, source_target_pairs={{64,0},{128,64},{192,128},{256,192},{320,256},{384,320},{448,384},... | collective-permute-start | bytes 1081352 | tf_op jit(solution)/shard_map/ppermute | solution.py:13
  332.6 111.0 %copy-start = (bf16[8,176,128]{2,1,0:T(8,128)(2,1)S(1)}, bf16[8,176,128]{2,1,0:T(8,128)(2,1)}, u32[]{:S(2)}) copy-start(bf16[8,176,128]{2,1,0:T(8,128)(2,1)} %get-tuple-element.90) | copy-start | bytes 1081348
  425.0 12.4 %all-to-all-start = ((f32[8,22,128]{2,1,0:T(8,128)}), f32[8,22,128]{2,1,0:T(8,128)S(1)}, u32[]{:S(2)}, u32[]{:S(2)}) async-start(f32[8,22,128]{2,1,0:T(8,128)} %all_to_all.24), calls=%async_computation.1 | async-start | bytes 196608 | tf_op jit(solution)/shard_map/all_to_all | solution.py:100
  437.4 9.6 %all-to-all-start.1 = ((f32[8,22,128]{2,1,0:T(8,128)}), f32[8,22,128]{2,1,0:T(8,128)S(1)}, u32[]{:S(2)}, u32[]{:S(2)}) async-start(f32[8,22,128]{2,1,0:T(8,128)} %all_to_all.27), calls=%async_computation.2 | async-start | bytes 196608 | tf_op jit(solution)/shard_map/all_to_all | solution.py:101
Sparse Core Ops, SparseCore 0:
  22.1 119.5 all-gather.6
  144.4 117.6 all-gather.4
  334.0 89.4 reduce-scatter.1
where the time goes:
time: 457 us; the launch traced here: 454 us
  waiting for transfers between devices  329 us (72%)
  matrix products  57.9 us (13%)
  starting transfers between devices  24.5 us (5%)
  local copies, waits for them, and re-layouts  19.7 us (4%)
  between operations  15.8 us (3%)
  other arithmetic  7.34 us (2%)
    all_gather x1, waiting for transfers between devices, body(): lax.all_gather(key_rows, ('ctx', 'tp'), axis=0, tiled=True)  119 us
    all_gather x1, waiting for transfers between devices, body(): lax.all_gather(value_rows, ('ctx', 'tp'), axis=0, tiled=True)  92.7 us
    reduce_scatter x1, waiting for transfers between devices, body(): lax.psum_scatter(grad_terms, 'ctx', scatter_dimension=0, tiled=True)  89.6 us
    ppermute x4, waiting for transfers between devices, passed_along(): return lax.ppermute(block, axis, route)  21.1 us
    ppermute x4, starting transfers between devices, passed_along(): return lax.ppermute(block, axis, route)  13.2 us
    dot_general x8, matrix products, per_head(): jnp.dot(dscores.T, q_one, preferred_element_type=jnp.float32) * scale  11.2 us
    dot_general x8, matrix products, per_head(): jnp.dot(probs_low.T, do_one, preferred_element_type=jnp.float32)  11 us
    dot_general x8, matrix products, per_head(): jnp.dot(q_one, key_head.T, preferred_element_type=jnp.float32) * scale  9.57 us
  transfers between devices with their start and end apart: 9, of which 9 were waited for; matrix products, arithmetic and copies ran while one was open for 2% of the time, Pallas kernels for 0%

commit v1 on v0

--- a/solution.py
+++ b/solution.py
@@ -38,7 +38,12 @@
     ).reshape(seq_rows)
     query_pos = lax.dynamic_slice_in_dim(positions, lax.axis_index("ctx") * tok_rows, tok_rows)
     key_full, value_full = (
-        lax.all_gather(key_rows, ("ctx", "tp"), axis=0, tiled=True),
+        jnp.concatenate(
+            lax.all_to_all(
+                jnp.stack([key_rows] * lax.axis_size(("ctx", "tp"))), ("ctx", "tp"), 0, 0
+            ),
+            axis=0,
+        ),
         lax.all_gather(value_rows, ("ctx", "tp"), axis=0, tiled=True),
     )
     key_store = lax.dynamic_slice_in_dim(key_full, tp_rank * kv_width, kv_width, 1)

time: 457 us -> 375 us (0.82)
  waiting for transfers between devices: 329 us -> 229 us
  starting transfers between devices: 24.5 us -> 36.1 us
  local copies, waits for them, and re-layouts: 19.7 us -> 26.5 us
    all_gather x1 -> x0, waiting for transfers between devices: 119 us -> none  [body(): lax.all_gather(key_rows, ('ctx', 'tp'), axis=0, tiled=True)]
    all_to_all x0 -> x1, waiting for transfers between devices: none -> 56.5 us  [body(): lax.all_to_all(jnp.stack([key_rows] * lax.axis_size(('ctx', 'tp'))), ('ct...]
    all_gather x1, waiting for transfers between devices: 92.7 us -> 54.1 us  [body(): lax.all_gather(value_rows, ('ctx', 'tp'), axis=0, tiled=True)]
    all_to_all x0 -> x1, starting transfers between devices: none -> 11.7 us  [body(): lax.all_to_all(jnp.stack([key_rows] * lax.axis_size(('ctx', 'tp'))), ('ct...]
    reshape x0 -> x1, local copies, waits for them, and re-layouts: none -> 5.36 us  [body(): jnp.concatenate(lax.all_to_all(jnp.stack([key_rows] * lax.axis_size(('ctx...]
  transfers between devices with their start and end apart: 9 -> 9, of which waited for: 9 -> 9; matrix products, arithmetic and copies ran while one was open for 2% -> 4% of each run, Pallas kernels for 0% -> 0%
where the time goes in v1:
time: 375 us; the launch traced here: 372 us
  waiting for transfers between devices  229 us (61%)
  matrix products  57.9 us (15%)
  starting transfers between devices  36.1 us (10%)
  local copies, waits for them, and re-layouts  26.5 us (7%)
  between operations  16.2 us (4%)
  other arithmetic  6.67 us (2%)
    reduce_scatter x1, waiting for transfers between devices, body(): lax.psum_scatter(grad_terms, 'ctx', scatter_dimension=0, tiled=True)  88.6 us
    all_to_all x1, waiting for transfers between devices, body(): lax.all_to_all(jnp.stack([key_rows] * lax.axis_size(('ctx', 'tp'))), ('ct...  56.5 us
    all_gather x1, waiting for transfers between devices, body(): lax.all_gather(value_rows, ('ctx', 'tp'), axis=0, tiled=True)  54.1 us
    ppermute x4, waiting for transfers between devices, passed_along(): return lax.ppermute(block, axis, route)  22.9 us
    ppermute x4, starting transfers between devices, passed_along(): return lax.ppermute(block, axis, route)  13.2 us
    all_to_all x1, starting transfers between devices, body(): lax.all_to_all(jnp.stack([key_rows] * lax.axis_size(('ctx', 'tp'))), ('ct...  11.7 us
    dot_general x8, matrix products, per_head(): jnp.dot(dscores.T, q_one, preferred_element_type=jnp.float32) * scale  11.2 us
    dot_general x8, matrix products, per_head(): jnp.dot(probs_low.T, do_one, preferred_element_type=jnp.float32)  11 us
  transfers between devices with their start and end apart: 9, of which 9 were waited for; matrix products, arithmetic and copies ran while one was open for 4% of the time, Pallas kernels for 0%

profile of v1, /device:TPU:1, one launch (start us, length us, event | category | flops | bytes accessed | tf_op | source)
XLA Modules:
  0.0 372.2 jit_solution(74936306192800214)
XLA Ops:
  8.1 4.8 %collective-permute-start.1 = (bf16[2,22,1024]{2,1,0:T(8,128)(2,1)S(1)}, bf16[2,22,1024]{2,1,0:T(8,128)(2,1)S(1)}, u32[]{:S(2)}, u32[]{:S(2)}) collective-permute-start(bf16[2,22,1024]{2,1,0:T(8,128)(2,1)S(1)} %bitcast.112), channel_id=1, source_target_pairs={{448,0},{0,64},{64,128},{128,192},{192,256},{256,320},{320,384},{3... | collective-permute-start | bytes 270344 | tf_op jit(solution)/shard_map/ppermute | solution.py:13
  16.1 6.0 %collective-permute-done.1 = bf16[2,22,1024]{2,1,0:T(8,128)(2,1)S(1)} collective-permute-done((bf16[2,22,1024]{2,1,0:T(8,128)(2,1)S(1)}, bf16[2,22,1024]{2,1,0:T(8,128)(2,1)S(1)}, u32[]{:S(2)}, u32[]{:S(2)}) %collective-permute-start.1) | collective-permute-done | bytes 90144 | tf_op jit(solution)/shard_map/ppermute | solution.py:13
  22.1 2.0 stack.2
  24.1 11.7 %all-to-all-start = ((bf16[64,22,1024]{2,1,0:T(8,128)(2,1)}), bf16[64,22,1024]{2,1,0:T(8,128)(2,1)}, u32[]{:S(2)}, u32[]{:S(2)}) async-start(bf16[64,22,1024]{2,1,0:T(8,128)(2,1)} %stack.2), calls=%async_computation | async-start | bytes 6291456 | tf_op jit(solution)/shard_map/all_to_all | solution.py:42
  35.8 1.9 collective-permute-start.3
  37.8 5.0 %collective-permute-done.3 = bf16[2,22,1024]{2,0,1:T(2,128)(2,1)S(1)} collective-permute-done((bf16[2,22,1024]{2,0,1:T(2,128)(2,1)S(1)}, bf16[2,22,1024]{2,0,1:T(2,128)(2,1)S(1)}, u32[]{:S(2)}, u32[]{:S(2)}) %collective-permute-start.3) | collective-permute-done | bytes 90144 | tf_op jit(solution)/shard_map/ppermute | solution.py:13
  43.5 1.9 collective-permute-start
  45.5 4.6 %collective-permute-start.2 = (bf16[176,1024]{1,0:T(8,128)(2,1)}, bf16[176,1024]{1,0:T(8,128)(2,1)S(1)}, u32[]{:S(2)}, u32[]{:S(2)}) collective-permute-start(bf16[176,1024]{1,0:T(8,128)(2,1)} %bitcast.6), channel_id=1, source_target_pairs={{64,0},{128,64},{192,128},{256,192},{320,256},{384,320},{448,384},... | collective-permute-start | bytes 1081352 | tf_op jit(solution)/shard_map/ppermute | solution.py:13
  50.4 6.2 %collective-permute-done.2 = bf16[176,1024]{1,0:T(8,128)(2,1)S(1)} collective-permute-done((bf16[176,1024]{1,0:T(8,128)(2,1)}, bf16[176,1024]{1,0:T(8,128)(2,1)S(1)}, u32[]{:S(2)}, u32[]{:S(2)}) %collective-permute-start.2) | collective-permute-done | bytes 360480 | tf_op jit(solution)/shard_map/ppermute | solution.py:13
  57.4 5.7 %collective-permute-done = bf16[2,176,1024]{2,1,0:T(8,128)(2,1)S(1)} collective-permute-done((bf16[2,176,1024]{2,1,0:T(8,128)(2,1)S(1)}, bf16[2,176,1024]{2,1,0:T(8,128)(2,1)S(1)}, u32[]{:S(2)}, u32[]{:S(2)}) %collective-permute-start) | collective-permute-done | bytes 720928 | tf_op jit(solution)/shard_map/ppermute | solution.py:13
  64.0 56.5 %all-to-all-done = bf16[64,22,1024]{2,1,0:T(8,128)(2,1)} async-done(((bf16[64,22,1024]{2,1,0:T(8,128)(2,1)}), bf16[64,22,1024]{2,1,0:T(8,128)(2,1)}, u32[]{:S(2)}, u32[]{:S(2)}) %all-to-all-start) | async-done | bytes 2883616 | tf_op jit(solution)/shard_map/all_to_all | solution.py:42
  120.5 5.4 %reshape.64 = bf16[1408,1024]{1,0:T(8,128)(2,1)} reshape(bf16[64,22,1024]{2,1,0:T(8,128)(2,1)} %all-to-all-done) | data formatting | bytes 5767168 | tf_op jit(solution)/shard_map/reshape | solution.py:41
  126.9 54.1 %all-gather.3.cloned.1.call-done = bf16[1,1408,1024]{2,0,1:T(2,128)(2,1)} async-done(((bf16[1,22,1024]{2,0,1:T(2,128)(2,1)}), bf16[1,1408,1024]{2,0,1:T(2,128)(2,1)}) %all-gather.3.cloned.1.call-update) | async-done | bytes 2883600 | tf_op jit(solution)/shard_map/all_gather | solution.py:47
  180.9 1.8 constant_dynamic-slice_fusion
  182.8 68.6 %while.30 = (s32[]{:T(128)}, f32[1408,128]{1,0:T(8,128)S(1)}, f32[1408,128]{1,0:T(8,128)S(1)}, bf16[8,176,128]{2,1,0:T(8,128)(2,1)}, bf16[8,176,128]{2,1,0:T(8,1...) while((s32[]{:T(128)}, f32[1408,128]{1,0:T(8,128)S(1)}, ...), condition=%wide.region_4.5_spmd.clone, body=%wide.region_0.4_spmd.clone.sunk | while | flops 386129568 | bytes 11705100 | solution.py:88
  187.0 1.4 fusion.65
  195.6 1.4 fusion.65
  204.2 1.4 fusion.65
  247.0 1.4 fusion.65
  252.6 88.6 %reduce-scatter.2.cloned.1.call-done = f32[176,256]{1,0:T(8,128)} async-done(((f32[1408,256]{1,0:T(8,128)}), f32[176,256]{1,0:T(8,128)}) %reduce-scatter.2.cloned.1.call-update) | async-done | bytes 180240 | tf_op jit(solution)/shard_map/reduce_scatter | solution.py:101
  342.8 6.9 %all-to-all-start.1 = ((f32[8,22,128]{2,1,0:T(8,128)}), f32[8,22,128]{2,1,0:T(8,128)S(1)}, u32[]{:S(2)}, u32[]{:S(2)}) async-start(f32[8,22,128]{2,1,0:T(8,128)} %all_to_all.28), calls=%async_computation.2 | async-start | bytes 196608 | tf_op jit(solution)/shard_map/all_to_all | solution.py:105
  350.4 4.8 %all-to-all-done.1 = f32[8,22,128]{2,1,0:T(8,128)S(1)} async-done(((f32[8,22,128]{2,1,0:T(8,128)}), f32[8,22,128]{2,1,0:T(8,128)S(1)}, u32[]{:S(2)}, u32[]{:S(2)}) %all-to-all-start.1) | async-done | bytes 90144 | tf_op jit(solution)/shard_map/all_to_all | solution.py:105
  355.1 4.2 %all-to-all-start.2 = ((f32[8,22,128]{2,1,0:T(8,128)}), f32[8,22,128]{2,1,0:T(8,128)S(1)}, u32[]{:S(2)}, u32[]{:S(2)}) async-start(f32[8,22,128]{2,1,0:T(8,128)} %all_to_all.31), calls=%async_computation.3 | async-start | bytes 196608 | tf_op jit(solution)/shard_map/all_to_all | solution.py:106
  363.0 1.8 all-to-all-done.2
  (117 shorter events, 76.4 us)
Async XLA Ops:
  8.1 14.0 %collective-permute-start.1 = (bf16[2,22,1024]{2,1,0:T(8,128)(2,1)S(1)}, bf16[2,22,1024]{2,1,0:T(8,128)(2,1)S(1)}, u32[]{:S(2)}, u32[]{:S(2)}) collective-permute-start(bf16[2,22,1024]{2,1,0:T(8,128)(2,1)S(1)} %bitcast.112), channel_id=1, source_target_pairs={{448,0},{0,64},{64,128},{128,192},{192,256},{256,320},{320,384},{3... | collective-permute-start | bytes 270344 | tf_op jit(solution)/shard_map/ppermute | solution.py:13
  24.1 11.7 %copy-start.2 = (bf16[1,2,22,1024]{3,1,2,0:T(2,128)(2,1)S(1)}, bf16[1,2,22,1024]{3,1,2,0:T(2,128)(2,1)}, u32[]{:S(2)}) copy-start(bf16[1,2,22,1024]{3,1,2,0:T(2,128)(2,1)} %param.12) | copy-start | bytes 270340
  24.1 19.4 %copy-start.1 = (bf16[1,2,176,1024]{3,2,1,0:T(8,128)(2,1)S(1)}, bf16[1,2,176,1024]{3,2,1,0:T(8,128)(2,1)}, u32[]{:S(2)}) copy-start(bf16[1,2,176,1024]{3,2,1,0:T(8,128)(2,1)} %param.10) | copy-start | bytes 2162692
  24.1 26.0 %copy-start.3 = (s32[16]{0:T(128)S(1)}, s32[16]{0:T(128)}, u32[]{:S(2)}) copy-start(s32[16]{0:T(128)} %param.8) | copy-start | bytes 196
  24.1 96.4 %all-to-all-start = ((bf16[64,22,1024]{2,1,0:T(8,128)(2,1)}), bf16[64,22,1024]{2,1,0:T(8,128)(2,1)}, u32[]{:S(2)}, u32[]{:S(2)}) async-start(bf16[64,22,1024]{2,1,0:T(8,128)(2,1)} %stack.2), calls=%async_computation | async-start | bytes 6291456 | tf_op jit(solution)/shard_map/all_to_all | solution.py:42
  35.8 145.2 %all-gather.3.cloned.1.call-start = ((), (), s32[]{:S(2)}) async-start(), calls=%async_computation.5 | async-start | bytes 5857280 | tf_op jit(solution)/shard_map/all_gather | solution.py:47
  35.8 6.9 %collective-permute-start.3 = (bf16[2,22,1024]{2,0,1:T(2,128)(2,1)S(1)}, bf16[2,22,1024]{2,0,1:T(2,128)(2,1)S(1)}, u32[]{:S(2)}, u32[]{:S(2)}) collective-permute-start(bf16[2,22,1024]{2,0,1:T(2,128)(2,1)S(1)} %bitcast.116), channel_id=1, source_target_pairs={{448,0},{0,64},{64,128},{128,192},{192,256},{256,320},{320,384},{3... | collective-permute-start | bytes 270344 | tf_op jit(solution)/shard_map/ppermute | solution.py:13
  43.5 297.7 %reduce-scatter.2.cloned.1.call-start = ((), (), s32[]{:S(2)}) async-start(), calls=%async_computation.4 | async-start | bytes 1622016 | tf_op jit(solution)/shard_map/reduce_scatter | solution.py:101
  43.5 19.6 %collective-permute-start = (bf16[2,176,1024]{2,1,0:T(8,128)(2,1)S(1)}, bf16[2,176,1024]{2,1,0:T(8,128)(2,1)S(1)}, u32[]{:S(2)}, u32[]{:S(2)}) collective-permute-start(bf16[2,176,1024]{2,1,0:T(8,128)(2,1)S(1)} %bitcast.115), channel_id=1, source_target_pairs={{448,0},{0,64},{64,128},{128,192},{192,256},{256,320},{320,384},{3... | collective-permute-start | bytes 2162696 | tf_op jit(solution)/shard_map/ppermute | solution.py:13
  45.5 11.1 %collective-permute-start.2 = (bf16[176,1024]{1,0:T(8,128)(2,1)}, bf16[176,1024]{1,0:T(8,128)(2,1)S(1)}, u32[]{:S(2)}, u32[]{:S(2)}) collective-permute-start(bf16[176,1024]{1,0:T(8,128)(2,1)} %bitcast.6), channel_id=1, source_target_pairs={{64,0},{128,64},{192,128},{256,192},{320,256},{384,320},{448,384},... | collective-permute-start | bytes 1081352 | tf_op jit(solution)/shard_map/ppermute | solution.py:13
  251.4 109.9 %copy-start = (bf16[8,176,128]{2,1,0:T(8,128)(2,1)S(1)}, bf16[8,176,128]{2,1,0:T(8,128)(2,1)}, u32[]{:S(2)}) copy-start(bf16[8,176,128]{2,1,0:T(8,128)(2,1)} %get-tuple-element.90) | copy-start | bytes 1081348
  342.8 12.3 %all-to-all-start.1 = ((f32[8,22,128]{2,1,0:T(8,128)}), f32[8,22,128]{2,1,0:T(8,128)S(1)}, u32[]{:S(2)}, u32[]{:S(2)}) async-start(f32[8,22,128]{2,1,0:T(8,128)} %all_to_all.28), calls=%async_computation.2 | async-start | bytes 196608 | tf_op jit(solution)/shard_map/all_to_all | solution.py:105
  355.1 9.6 %all-to-all-start.2 = ((f32[8,22,128]{2,1,0:T(8,128)}), f32[8,22,128]{2,1,0:T(8,128)S(1)}, u32[]{:S(2)}, u32[]{:S(2)}) async-start(f32[8,22,128]{2,1,0:T(8,128)} %all_to_all.31), calls=%async_computation.3 | async-start | bytes 196608 | tf_op jit(solution)/shard_map/all_to_all | solution.py:106
Sparse Core Ops, SparseCore 0:
  43.6 137.2 all-gather.2
  252.7 88.4 reduce-scatter.1
